TPU v7x, 256 devices: a whole 4x4x8 slice. The times are simulated.
256 devices in a mesh: ctx: 16 (over z, core), tp: 16 (over x, y).
Axes of the slice: x: 4, y: 4, z: 8, core: 2. Of those that a mesh axis runs over, the one named last changes fastest.
Arguments:
- q_act: bfloat16 [64, 128, 4096], P('ctx', None, 'tp'), may hold values from -16 to 16
- k_act: bfloat16 [64, 128, 4096], P('ctx', None, 'tp'), may hold values from -16 to 16
- v_act: bfloat16 [64, 128, 4096], P('ctx', None, 'tp'), may hold values from -6 to 6
- grad_out: bfloat16 [8192, 4096], P(('ctx', 'tp')), may hold values from -24 to 24
- w_out: bfloat16 [4096, 4096], P(None, 'tp'), may hold values from -0.09375 to 0.09375
- nbr_tiles: int32 [64, 12], replicated, may hold values from 0 to 63, as said below
- nbr_valid: int32 [64, 12], replicated, may hold values from 0 to 1, as said below
- slot_of: int32 [64], replicated, may hold values from 0 to 63, as said below
Outputs:
- grad_q: bfloat16 [64, 128, 4096], P('ctx', None, 'tp')
- grad_k: bfloat16 [64, 128, 4096], P('ctx', None, 'tp')
- grad_v: bfloat16 [64, 128, 4096], P('ctx', None, 'tp')
- grad_w_out: bfloat16 [4096, 4096], P('ctx', 'tp')
Inputs may be any that keep to these rules, and one draw needn't show every extreme that they name: `nbr_tiles`: row t lists scenario tiles linked to tile t; the live entries of a row name distinct tiles, one of them t itself. `nbr_valid`: every row has at least one live entry; a tile is named by live entries of at most 12 rows. `slot_of`: a permutation; slots c * 4 to c * 4 + 3 are held by index c of ctx.
All inputs are finite; a program needn't handle non-finite values.
Results may differ from a plain program's by a relative error of at most 0.024.
Values may be sent and summed in bfloat16 or wider, within the bound.
No kernel may reach another device: no remote copies, remote signals or barrier semaphores. Data moves between devices by JAX's collectives and lax.ppermute only.
A program may use at most 128 MiB of HBM per device.

v0:
```python
import math
import jax
import jax.numpy as jnp
from jax import lax
from jax.sharding import PartitionSpec as P

HD = 128


def side_by_side(arrays, axis, dim, along):
    widths = [a.shape[along] for a in arrays]
    both = jnp.concatenate(arrays, axis=along)
    out = lax.all_gather(both, axis, axis=dim, tiled=True)
    return tuple(jnp.split(out, [sum(widths[:k]) for k in range(1, len(widths))], axis=along))


def slot_tables(nbr_tiles, nbr_valid, slot_of):
    tile_count = slot_of.shape[0]
    slot_index = jnp.arange(tile_count, dtype=jnp.int32)
    matches = (slot_of[:, None] == slot_index[None, :]).astype(jnp.int32)
    near_tiles = jnp.einsum("ts,tj->sj", matches, nbr_tiles)
    live_mask = jnp.einsum("ts,tj->sj", matches, nbr_valid)
    found = (near_tiles[:, :, None] == slot_index[None, None, :]).astype(jnp.int32)
    key_slot = jnp.sum(found * slot_of[None, None, :], axis=2)
    return (key_slot, live_mask)


def per_device(q_act, k_act, v_act, grad_out, w_out, nbr_tiles, nbr_valid, slot_of):
    local_tiles, tile_len, col_width = q_act.shape
    head_count = col_width // HD
    score_scale = 1.0 / math.sqrt(HD)
    ctx_count = lax.axis_size("ctx")
    tile_count = local_tiles * ctx_count
    first_slot = lax.axis_index("ctx") * local_tiles
    key_slot, live_mask = slot_tables(nbr_tiles, nbr_valid, slot_of)
    near_slots = lax.dynamic_slice_in_dim(key_slot, first_slot, local_tiles, 0)
    near_live = lax.dynamic_slice_in_dim(live_mask, first_slot, local_tiles, 0)
    list_len = near_slots.shape[1]
    full_rows = lax.all_gather(grad_out, "tp", axis=0, tiled=True)
    grad_flat = jnp.dot(full_rows, w_out, preferred_element_type=jnp.float32).astype(jnp.bfloat16)
    grad_tiles = grad_flat.reshape(local_tiles, tile_len, col_width)
    grad_grid = grad_flat.reshape(local_tiles, tile_len, head_count, HD)
    key_all, value_all = side_by_side((k_act, v_act), "ctx", 0, 1)
    near_keys = key_all[near_slots].reshape(local_tiles, list_len, tile_len, head_count, HD)
    near_values = value_all[near_slots].reshape(local_tiles, list_len, tile_len, head_count, HD)
    query_grid = q_act.reshape(local_tiles, tile_len, head_count, HD)
    live_cells = (near_live > 0)[:, None, None, :, None]
    scores = (
        jnp.einsum("sahd,sjbhd->shajb", query_grid, near_keys, preferred_element_type=jnp.float32)
        * score_scale
    )
    row_peak = jnp.max(jnp.where(live_cells, scores, -1e30), axis=(3, 4), keepdims=True)
    row_total = jnp.sum(
        jnp.where(live_cells, jnp.exp(scores - row_peak), 0.0), axis=(3, 4), keepdims=True
    )
    log_total = row_peak + jnp.log(row_total)
    prob_full = jnp.where(live_cells, jnp.exp(scores - log_total), 0.0)
    prob_half = prob_full.astype(jnp.bfloat16)
    attn_grid = jnp.einsum(
        "shajb,sjbhd->sahd", prob_half, near_values, preferred_element_type=jnp.float32
    ).astype(jnp.bfloat16)
    row_delta = jnp.einsum(
        "sahd,sahd->sha", grad_grid, attn_grid, preferred_element_type=jnp.float32
    )
    grad_prob = jnp.einsum(
        "sahd,sjbhd->shajb", grad_grid, near_values, preferred_element_type=jnp.float32
    )
    grad_score = (prob_full * (grad_prob - row_delta[:, :, :, None, None])).astype(jnp.bfloat16)
    grad_query = (
        jnp.einsum("shajb,sjbhd->sahd", grad_score, near_keys, preferred_element_type=jnp.float32)
        * score_scale
    )
    grad_q = grad_query.astype(jnp.bfloat16).reshape(local_tiles, tile_len, col_width)
    query_all, grad_all = (
        lax.all_gather(q_act, "ctx", axis=0, tiled=True),
        lax.all_gather(grad_tiles, "ctx", axis=0, tiled=True),
    )
    total_all, delta_all = side_by_side((log_total[:, :, :, 0, 0], row_delta), "ctx", 0, 1)
    query_wide = query_all.reshape(tile_count, tile_len, head_count, HD)
    grad_wide = grad_all.reshape(tile_count, tile_len, head_count, HD)
    owned_slots = first_slot + jnp.arange(local_tiles, dtype=jnp.int32)
    pair_hits = (key_slot[:, :, None] == owned_slots[None, None, :]) & (live_mask[:, :, None] > 0)
    named_by = jnp.any(pair_hits, axis=1).astype(jnp.int32)
    rank_of = jnp.cumsum(named_by, axis=0) - 1
    list_pos = jnp.arange(list_len, dtype=jnp.int32)
    placed = (named_by[:, :, None] > 0) & (rank_of[:, :, None] == list_pos[None, None, :])
    slot_index = jnp.arange(tile_count, dtype=jnp.int32)
    picked = jnp.sum(placed.astype(jnp.int32) * slot_index[:, None, None], axis=0)
    picked_live = jnp.any(placed, axis=0)

    def owner_grads(inputs):
        key_tile, value_tile, chosen, chosen_live = inputs
        query_rows = query_wide[chosen]
        grad_rows = grad_wide[chosen]
        total_rows = total_all[chosen]
        delta_rows = delta_all[chosen]
        owner_scores = (
            jnp.einsum("tahd,bhd->thab", query_rows, key_tile, preferred_element_type=jnp.float32)
            * score_scale
        )
        keep_pair = chosen_live[:, None, None, None]
        owner_probs = jnp.where(keep_pair, jnp.exp(owner_scores - total_rows[:, :, :, None]), 0.0)
        owner_grad_prob = jnp.einsum(
            "tahd,bhd->thab", grad_rows, value_tile, preferred_element_type=jnp.float32
        )
        owner_grad_score = (owner_probs * (owner_grad_prob - delta_rows[:, :, :, None])).astype(
            jnp.bfloat16
        )
        grad_key = (
            jnp.einsum(
                "thab,tahd->bhd", owner_grad_score, query_rows, preferred_element_type=jnp.float32
            )
            * score_scale
        )
        grad_value = jnp.einsum(
            "thab,tahd->bhd",
            owner_probs.astype(jnp.bfloat16),
            grad_rows,
            preferred_element_type=jnp.float32,
        )
        return (grad_key.astype(jnp.bfloat16), grad_value.astype(jnp.bfloat16))

    key_local = k_act.reshape(local_tiles, tile_len, head_count, HD)
    value_local = v_act.reshape(local_tiles, tile_len, head_count, HD)
    grad_key_all, grad_value_all = lax.map(
        owner_grads, (key_local, value_local, picked, picked_live)
    )
    grad_k = grad_key_all.reshape(local_tiles, tile_len, col_width)
    grad_v = grad_value_all.reshape(local_tiles, tile_len, col_width)
    attn_flat = attn_grid.reshape(local_tiles * tile_len, col_width)
    grad_weight = lax.psum_scatter(
        lax.dot_general(
            full_rows, attn_flat, (((0,), (0,)), ((), ())), preferred_element_type=jnp.float32
        ).astype(jnp.bfloat16),
        "ctx",
        scatter_dimension=0,
        tiled=True,
    )
    return (grad_q, grad_k, grad_v, grad_weight)


def solution(mesh):
    in_specs = (
        P("ctx", None, "tp"),
        P("ctx", None, "tp"),
        P("ctx", None, "tp"),
        P(("ctx", "tp"), None),
        P(None, "tp"),
        P(),
        P(),
        P(),
    )
    out_specs = (P("ctx", None, "tp"), P("ctx", None, "tp"), P("ctx", None, "tp"), P("ctx", "tp"))
    return jax.shard_map(
        per_device, mesh=mesh, in_specs=in_specs, out_specs=out_specs, check_vma=False
    )
```

profile of v0, /device:TPU:1, one launch (start us, length us, event | category | flops | bytes accessed | tf_op | source)
XLA Modules:
  0.0 342.1 jit_solution(13095757694921598269)
XLA Ops:
  8.7 1.9 pad_maximum_fusion
  10.8 59.7 %all-gather.7.cloned.1.call-done = bf16[512,4096]{1,0:T(8,128)(2,1)} async-done(((bf16[32,4096]{1,0:T(8,128)(2,1)}), bf16[512,4096]{1,0:T(8,128)(2,1)}) %all-gather.7.cloned.1.call-update) | async-done | bytes 4194320 | tf_op jit(solution)/shard_map/all_gather | solution.py:39
  70.5 4.1 %convolution_convert_fusion.1 = bf16[512,256]{1,0:T(8,128)(2,1)} fusion(bf16[512,4096]{1,0:T(8,128)(2,1)} %all-gather.7.cloned.1.call-done, bf16[4096,256]{1,0:T(8,128)(2,1)S(1)} %copy-done), kind=kOutput, calls=%fused_computation.56 | convolution fusion | flops 1073872896 | bytes 6553600 | tf_op jit(solution)/shard_map/dot_general | solution.py:40
  81.3 33.3 %all-gather.9.cloned.1.call-done = bf16[64,128,256]{2,1,0:T(8,128)(2,1)} async-done(((bf16[4,128,256]{2,1,0:T(8,128)(2,1)}), bf16[64,128,256]{2,1,0:T(8,128)(2,1)}) %all-gather.9.cloned.1.call-update) | async-done | bytes 4194320 | tf_op jit(solution)/shard_map/all_gather | solution.py:75
  114.5 6.9 %reshape.119 = bf16[64,128,2,128]{3,2,1,0:T(2,128)(2,1)} reshape(bf16[64,128,256]{2,1,0:T(8,128)(2,1)} %all-gather.9.cloned.1.call-done) | data formatting | bytes 8388608 | tf_op jit(solution)/shard_map/reshape | solution.py:79
  121.5 49.4 %all-gather.5.cloned.1.call-done = bf16[64,256,256]{2,1,0:T(8,128)(2,1)} async-done(((bf16[4,256,256]{2,1,0:T(8,128)(2,1)}), bf16[64,256,256]{2,1,0:T(8,128)(2,1)}) %all-gather.5.cloned.1.call-update) | async-done | bytes 8388624 | tf_op jit(solution)/shard_map/all_gather | solution.py:13
  170.8 6.0 %fusion.65 = (bf16[64,128,256]{2,1,0:T(8,128)(2,1)}, bf16[64,128,256]{2,1,0:T(8,128)(2,1)}) fusion(bf16[64,256,256]{2,1,0:T(8,128)(2,1)} %all-gather.5.cloned.1.call-done), kind=kLoop, calls=%fused_computation.91 | loop fusion | bytes 16777216 | tf_op jit(solution)/shard_map/split | solution.py:14
  176.9 2.9 gather_fusion.4
  179.8 3.0 reshape.114
  182.8 7.2 %copy.136 = bf16[4,12,128,2,128]{2,4,1,3,0:T(8,128)(2,1)S(1)} copy(bf16[4,12,128,2,128]{4,3,2,1,0:T(2,128)(2,1)} %reshape.114) | data formatting | bytes 6291456 | tf_op jit(solution)/shard_map/reshape | solution.py:44
  190.1 4.7 %gather_fusion.5 = bf16[48,128,256]{2,1,0:T(8,128)(2,1)} fusion(bf16[64,128,256]{2,1,0:T(8,128)(2,1)} %get-tuple-element.150, s32[1024]{0:T(1024)S(1)} %pad_clamp_fusion.1), kind=kCustom, calls=%fused_computation.5 | custom fusion | bytes 6291648 | tf_op jit(solution)/shard_map/gather | solution.py:45
  194.8 5.5 %reshape.117 = bf16[4,12,128,2,128]{4,3,2,1,0:T(2,128)(2,1)} reshape(bf16[48,128,256]{2,1,0:T(8,128)(2,1)} %gather_fusion.5) | data formatting | bytes 6291456 | tf_op jit(solution)/shard_map/reshape | solution.py:45
  200.3 8.6 %copy.133 = bf16[4,12,128,2,128]{2,4,1,3,0:T(8,128)(2,1)} copy(bf16[4,12,128,2,128]{4,3,2,1,0:T(2,128)(2,1)} %reshape.117) | data formatting | bytes 6291456 | tf_op jit(solution)/shard_map/reshape | solution.py:45
  209.0 1.9 select_reduce_fusion.1
  210.9 1.4 select_reduce_fusion
  212.3 1.8 copy-done.2
  215.1 2.4 multiply_reduce_fusion
  217.6 7.6 %fusion.45 = bf16[4,2,128,128]{3,2,1,0:T(8,128)(2,1)} fusion(bf16[4,12,128,2,128]{2,4,1,3,0:T(8,128)(2,1)S(1)} %copy.136, f32[4,2,12,128,128]{4,3,2,1,0:T(8,128)} %copy-done.2, f32[4,2,128]{2,1,0:T(2,128)S(1)} %get-tuple-element.160, f32[4,2,128]{2,1,0:T(2,128)S(1)} %bitcast.194, pred[4,12]{1,0:T(4,128)(4,1)S(1)} %copy.128, ...), kind=kOutput, calls=%fused_computation.55 | convolution fusion | flops 815005696 | bytes 13115440 | tf_op jit(solution)/shard_map/shajb,sjbhd->sahd/dot_general | solution.py:70
  225.1 1.8 copy.149
  228.0 16.2 %all_gather.18 = f32[64,4,128]{2,1,0:T(4,128)S(1)} all-gather(f32[4,4,128]{2,1,0:T(4,128)S(1)} %pad_maximum_fusion.1), channel_id=1, replica_groups=mesh['ctx'=16,'tp'=16] {'ctx'}, dimensions={0}, use_global_device_ids=true | all-gather | bytes 139264 | tf_op jit(solution)/shard_map/all_gather | solution.py:13
  244.9 4.8 %fusion.27 = bf16[4096,256]{0,1:T(8,128)(2,1)} fusion(bf16[512,4096]{1,0:T(8,128)(2,1)} %all-gather.7.cloned.1.call-done, bf16[64,8,2,128]{3,2,1,0:T(2,128)(2,1)S(1)} %bitcast.185), kind=kOutput, calls=%fused_computation.43 | convolution fusion | flops 1074790400 | bytes 6553600 | tf_op jit(solution)/shard_map/dot_general | solution.py:132
  249.8 7.0 %reshape.123 = bf16[64,128,2,128]{3,2,1,0:T(2,128)(2,1)} reshape(bf16[64,128,256]{2,1,0:T(8,128)(2,1)} %all-gather.11.cloned.1.call-done) | data formatting | bytes 8388608 | tf_op jit(solution)/shard_map/reshape | solution.py:80
  256.7 74.5 %while.12 = (s32[]{:T(128)}, bf16[4,128,2,128]{1,3,2,0:T(8,128)(2,1)S(1)}, bf16[4,128,2,128]{1,3,2,0:T(8,128)(2,1)}, s32[4,12]{1,0:T(4,128)S(1)}, bf16[64,128,2,...) while((s32[]{:T(128)}, ...), condition=%wide.region_8.9_spmd, body=%wide.region_7.8_spmd.sunk | while | flops 405505056 | bytes 14550529 | solution.py:125
  256.8 4.3 %gather_fusion = bf16[12,128,2,128]{3,2,1,0:T(2,128)(2,1)S(1)} fusion(bf16[64,128,2,128]{3,2,1,0:T(2,128)(2,1)} %get-tuple-element.257, s32[1024]{0:T(1024)S(1)} %pad_clamp_fusion.3), kind=kCustom, calls=%fused_computation.clone.1 | custom fusion | bytes 1572912 | tf_op jit(solution)/shard_map/while/body/eval_jaxpr/gather | solution.py:93
  261.8 1.4 gather_fusion.1
  263.2 1.3 fusion.99
  264.6 5.3 %gather_fusion.2 = bf16[12,128,2,128]{3,2,1,0:T(2,128)(2,1)} fusion(bf16[64,128,2,128]{3,2,1,0:T(2,128)(2,1)} %get-tuple-element.262, s32[1024]{0:T(1024)S(1)} %pad_clamp_fusion.3), kind=kCustom, calls=%fused_computation.2.clone.1 | custom fusion | bytes 1572912 | tf_op jit(solution)/shard_map/while/body/eval_jaxpr/gather | solution.py:94
  269.9 2.3 copy.196
  272.8 1.5 fusion.100
  275.4 4.3 %gather_fusion = bf16[12,128,2,128]{3,2,1,0:T(2,128)(2,1)S(1)} fusion(bf16[64,128,2,128]{3,2,1,0:T(2,128)(2,1)} %get-tuple-element.257, s32[1024]{0:T(1024)S(1)} %pad_clamp_fusion.3), kind=kCustom, calls=%fused_computation.clone.1 | custom fusion | bytes 1572912 | tf_op jit(solution)/shard_map/while/body/eval_jaxpr/gather | solution.py:93
  280.4 1.4 gather_fusion.1
  281.9 1.3 fusion.99
  283.2 5.3 %gather_fusion.2 = bf16[12,128,2,128]{3,2,1,0:T(2,128)(2,1)} fusion(bf16[64,128,2,128]{3,2,1,0:T(2,128)(2,1)} %get-tuple-element.262, s32[1024]{0:T(1024)S(1)} %pad_clamp_fusion.3), kind=kCustom, calls=%fused_computation.2.clone.1 | custom fusion | bytes 1572912 | tf_op jit(solution)/shard_map/while/body/eval_jaxpr/gather | solution.py:94
  288.6 2.3 copy.196
  291.5 1.5 fusion.100
  294.0 4.3 %gather_fusion = bf16[12,128,2,128]{3,2,1,0:T(2,128)(2,1)S(1)} fusion(bf16[64,128,2,128]{3,2,1,0:T(2,128)(2,1)} %get-tuple-element.257, s32[1024]{0:T(1024)S(1)} %pad_clamp_fusion.3), kind=kCustom, calls=%fused_computation.clone.1 | custom fusion | bytes 1572912 | tf_op jit(solution)/shard_map/while/body/eval_jaxpr/gather | solution.py:93
  299.1 1.4 gather_fusion.1
  300.5 1.3 fusion.99
  301.8 5.3 %gather_fusion.2 = bf16[12,128,2,128]{3,2,1,0:T(2,128)(2,1)} fusion(bf16[64,128,2,128]{3,2,1,0:T(2,128)(2,1)} %get-tuple-element.262, s32[1024]{0:T(1024)S(1)} %pad_clamp_fusion.3), kind=kCustom, calls=%fused_computation.2.clone.1 | custom fusion | bytes 1572912 | tf_op jit(solution)/shard_map/while/body/eval_jaxpr/gather | solution.py:94
  307.2 2.3 copy.196
  310.1 1.5 fusion.100
  312.6 4.3 %gather_fusion = bf16[12,128,2,128]{3,2,1,0:T(2,128)(2,1)S(1)} fusion(bf16[64,128,2,128]{3,2,1,0:T(2,128)(2,1)} %get-tuple-element.257, s32[1024]{0:T(1024)S(1)} %pad_clamp_fusion.3), kind=kCustom, calls=%fused_computation.clone.1 | custom fusion | bytes 1572912 | tf_op jit(solution)/shard_map/while/body/eval_jaxpr/gather | solution.py:93
  317.7 1.4 gather_fusion.1
  320.5 5.3 %gather_fusion.2 = bf16[12,128,2,128]{3,2,1,0:T(2,128)(2,1)} fusion(bf16[64,128,2,128]{3,2,1,0:T(2,128)(2,1)} %get-tuple-element.262, s32[1024]{0:T(1024)S(1)} %pad_clamp_fusion.3), kind=kCustom, calls=%fused_computation.2.clone.1 | custom fusion | bytes 1572912 | tf_op jit(solution)/shard_map/while/body/eval_jaxpr/gather | solution.py:94
  325.8 2.3 copy.196
  328.7 1.5 fusion.100
  332.1 1.8 copy.175
  333.9 1.7 copy.150
  (105 shorter events, 22.5 us)
Async XLA Ops:
  7.2 63.3 %copy-start = (bf16[4096,256]{1,0:T(8,128)(2,1)S(1)}, bf16[4096,256]{1,0:T(8,128)(2,1)}, u32[]{:S(2)}) copy-start(bf16[4096,256]{1,0:T(8,128)(2,1)} %param.14) | copy-start | bytes 6291460
  7.2 63.3 %all-gather.7.cloned.1.call-start = ((), (), s32[]{:S(2)}) async-start(), calls=%async_computation.2 | async-start | bytes 4456448 | tf_op jit(solution)/shard_map/all_gather | solution.py:39
  7.9 106.6 %all-gather.9.cloned.1.call-start = ((), (), s32[]{:S(2)}) async-start(), calls=%async_computation.3 | async-start | bytes 4456448 | tf_op jit(solution)/shard_map/all_gather | solution.py:75
  8.7 162.2 %all-gather.5.cloned.1.call-start = ((), (), s32[]{:S(2)}) async-start(), calls=%async_computation.1 | async-start | bytes 8912896 | tf_op jit(solution)/shard_map/all_gather | solution.py:13
  10.6 64.1 %copy-start.6 = (bf16[4,128,256]{2,1,0:T(8,128)(2,1)S(1)}, bf16[4,128,256]{2,1,0:T(8,128)(2,1)}, u32[]{:S(2)}) copy-start(bf16[4,128,256]{2,1,0:T(8,128)(2,1)} %param.10) | copy-start | bytes 786436
  10.7 64.2 %copy-start.7 = (bf16[4,128,256]{2,1,0:T(8,128)(2,1)S(1)}, bf16[4,128,256]{2,1,0:T(8,128)(2,1)}, u32[]{:S(2)}) copy-start(bf16[4,128,256]{2,1,0:T(8,128)(2,1)} %param.11) | copy-start | bytes 786436
  10.7 65.0 %copy-start.8 = (bf16[4,128,256]{2,1,0:T(8,128)(2,1)S(1)}, bf16[4,128,256]{2,1,0:T(8,128)(2,1)}, u32[]{:S(2)}) copy-start(bf16[4,128,256]{2,1,0:T(8,128)(2,1)} %param.12) | copy-start | bytes 786436
  10.7 65.9 %copy-start.11 = (s32[64]{0:T(128)S(1)}, s32[64]{0:T(128)}, u32[]{:S(2)}) copy-start(s32[64]{0:T(128)} %param.17) | copy-start | bytes 772
  10.7 65.9 %copy-start.12 = (s32[64,12]{0,1:T(8,128)S(1)}, s32[64,12]{0,1:T(8,128)}, u32[]{:S(2)}) copy-start(s32[64,12]{0,1:T(8,128)} %param.15) | copy-start | bytes 9220
  10.7 66.7 %copy-start.13 = (s32[64,12]{0,1:T(8,128)S(1)}, s32[64,12]{0,1:T(8,128)}, u32[]{:S(2)}) copy-start(s32[64,12]{0,1:T(8,128)} %param.16) | copy-start | bytes 9220
  10.7 239.1 %all-gather.11.cloned.1.call-start = ((), (), s32[]{:S(2)}) async-start(), calls=%async_computation.4 | async-start | bytes 4456448 | tf_op jit(solution)/shard_map/all_gather | solution.py:76
  74.7 259.2 %reduce-scatter.2.cloned.1.call-start = ((), (), s32[]{:S(2)}) async-start(), calls=%async_computation.5 | async-start | bytes 2228224 | tf_op jit(solution)/shard_map/reduce_scatter | solution.py:131
  80.1 41.4 %copy-start.4 = (bf16[4,128,2,128]{3,2,1,0:T(2,128)(2,1)}, bf16[4,128,2,128]{3,2,1,0:T(2,128)(2,1)S(1)}, u32[]{:S(2)}) copy-start(bf16[4,128,2,128]{3,2,1,0:T(2,128)(2,1)S(1)} %reshape.116) | copy-start | bytes 786436
  210.9 3.2 copy-start.2
  210.9 4.2 %copy-start.3 = (bf16[4,12,128,2,128]{2,4,1,3,0:T(8,128)(2,1)S(1)}, bf16[4,12,128,2,128]{2,4,1,3,0:T(8,128)(2,1)}, u32[]{:S(2)}) copy-start(bf16[4,12,128,2,128]{2,4,1,3,0:T(8,128)(2,1)} %copy.133) | copy-start | bytes 9437188
  210.9 4.2 %copy-start.9 = (f32[4,2,128,128]{2,3,1,0:T(8,128)S(1)}, f32[4,2,128,128]{2,3,1,0:T(8,128)}, u32[]{:S(2)}) copy-start(f32[4,2,128,128]{2,3,1,0:T(8,128)} %copy.167) | copy-start | bytes 1572868
  215.1 2.4 copy-start.5
  249.7 7.0 %copy-start.10 = (bf16[4,128,2,128]{1,3,2,0:T(8,128)(2,1)S(1)}, bf16[4,128,2,128]{1,3,2,0:T(8,128)(2,1)}, u32[]{:S(2)}) copy-start(bf16[4,128,2,128]{1,3,2,0:T(8,128)(2,1)} %custom-call.12) | copy-start | bytes 786436
  331.2 4.3 %copy-start.1 = (bf16[4096,256]{1,0:T(8,128)(2,1)S(1)}, bf16[4096,256]{1,0:T(8,128)(2,1)}, u32[]{:S(2)}) copy-start(bf16[4096,256]{1,0:T(8,128)(2,1)} %param.14) | copy-start | bytes 6291460
Sparse Core Ops, SparseCore 0:
  10.4 60.0 all-gather.6
  72.3 42.1 all-gather.8
  116.4 54.3 all-gather.4
  173.1 40.4 all-gather.10
  249.9 56.4 reduce-scatter.1
where the time goes:
time: 344 us; the launch traced here: 342 us
  waiting for transfers between devices  144 us (42%)
  local copies, waits for them, and re-layouts  126 us (37%)
  matrix products  36.7 us (11%)
  blocking collectives  16.2 us (5%)
  between operations  14 us (4%)
  other arithmetic  4.96 us (1%)
    all_gather x1, waiting for transfers between devices, per_device(): full_rows = lax.all_gather(grad_out, 'tp', axis=0, tiled=True)  59.7 us
    all_gather x1, waiting for transfers between devices, side_by_side(): out = lax.all_gather(both, axis, axis=dim, tiled=True)  49.4 us
    all_gather x1, waiting for transfers between devices, per_device(): lax.all_gather(q_act, 'ctx', axis=0, tiled=True)  33.3 us
    gather x8, local copies, waits for them, and re-layouts, owner_grads(): grad_rows = grad_wide[chosen]  30.6 us
    gather x8, local copies, waits for them, and re-layouts, owner_grads(): query_rows = query_wide[chosen]  20.1 us
    all_gather x1, blocking collectives, side_by_side(): out = lax.all_gather(both, axis, axis=dim, tiled=True)  16.2 us
    reshape x2, local copies, waits for them, and re-layouts, per_device(): value_all[near_slots]  14.2 us
    reshape x2, local copies, waits for them, and re-layouts, per_device(): key_all[near_slots].reshape(local_tiles, list_len, tile_len, head_count, HD)  10.3 us
  transfers between devices with their start and end apart: 5, of which 3 were waited for; matrix products, arithmetic and copies ran while one was open for 48% of the time, Pallas kernels for 0%

commit v1 on v0

--- a/solution.py
+++ b/solution.py
@@ -3,6 +3,7 @@
 import jax.numpy as jnp
 from jax import lax
 from jax.sharding import PartitionSpec as P
+from jax.lax import all_to_all, psum
 
 HD = 128
 
@@ -71,8 +72,21 @@
         * score_scale
     )
     grad_q = grad_query.astype(jnp.bfloat16).reshape(local_tiles, tile_len, col_width)
+
+    def try_all_skins(block_here, along_axis):
+        parts_n = psum(1, axis_name=along_axis)
+        pieces_in = [parts_n if to_i == 0 else 1 for to_i in range(block_here.ndim)]
+        formed = all_to_all(
+            jnp.tile(block_here, pieces_in),
+            axis_name=along_axis,
+            split_axis=0,
+            concat_axis=0,
+            tiled=True,
+        )
+        return formed
+
     query_all, grad_all = (
-        lax.all_gather(q_act, "ctx", axis=0, tiled=True),
+        try_all_skins(q_act, "ctx"),
         lax.all_gather(grad_tiles, "ctx", axis=0, tiled=True),
     )
     total_all, delta_all = side_by_side((log_total[:, :, :, 0, 0], row_delta), "ctx", 0, 1)

time: 344 us -> 332 us (0.965)
  waiting for transfers between devices: 144 us -> 118 us
  starting transfers between devices: 0.2 us -> 10.1 us
  local copies, waits for them, and re-layouts: 126 us -> 130 us
    all_to_all x0 -> x1, waiting for transfers between devices: none -> 52.1 us  [try_all_skins(): all_to_all(jnp.tile(block_here, pieces_in), axis_name=along_axis, split_a...]
    all_gather x1 -> x0, waiting for transfers between devices: 33.3 us -> none  [per_device(): lax.all_gather(q_act, 'ctx', axis=0, tiled=True)]
    all_gather x1, waiting for transfers between devices: 49.4 us -> 18 us  [side_by_side(): out = lax.all_gather(both, axis, axis=dim, tiled=True)]
    all_gather x1, waiting for transfers between devices: 59.7 us -> 47 us  [per_device(): full_rows = lax.all_gather(grad_out, 'tp', axis=0, tiled=True)]
    all_to_all x0 -> x1, starting transfers between devices: none -> 9.97 us  [try_all_skins(): all_to_all(jnp.tile(block_here, pieces_in), axis_name=along_axis, split_a...]
  transfers between devices with their start and end apart: 5 -> 5, of which waited for: 3 -> 3; matrix products, arithmetic and copies ran while one was open for 48% -> 51% of each run, Pallas kernels for 0% -> 0%
where the time goes in v1:
time: 332 us; the launch traced here: 330 us
  local copies, waits for them, and re-layouts  130 us (39%)
  waiting for transfers between devices  118 us (36%)
  matrix products  36.7 us (11%)
  blocking collectives  16.2 us (5%)
  between operations  14 us (4%)
  starting transfers between devices  10.1 us (3%)
  other arithmetic  4.96 us (1%)
    all_to_all x1, waiting for transfers between devices, try_all_skins(): all_to_all(jnp.tile(block_here, pieces_in), axis_name=along_axis, split_a...  52.1 us
    all_gather x1, waiting for transfers between devices, per_device(): full_rows = lax.all_gather(grad_out, 'tp', axis=0, tiled=True)  47 us
    gather x8, local copies, waits for them, and re-layouts, owner_grads(): grad_rows = grad_wide[chosen]  30.6 us
    gather x8, local copies, waits for them, and re-layouts, owner_grads(): query_rows = query_wide[chosen]  20.1 us
    all_gather x1, waiting for transfers between devices, side_by_side(): out = lax.all_gather(both, axis, axis=dim, tiled=True)  18 us
    all_gather x1, blocking collectives, side_by_side(): out = lax.all_gather(both, axis, axis=dim, tiled=True)  16.2 us
    reshape x2, local copies, waits for them, and re-layouts, per_device(): value_all[near_slots]  14.3 us
    reshape x2, local copies, waits for them, and re-layouts, per_device(): key_all[near_slots].reshape(local_tiles, list_len, tile_len, head_count, HD)  10.3 us
  transfers between devices with their start and end apart: 5, of which 3 were waited for; matrix products, arithmetic and copies ran while one was open for 51% of the time, Pallas kernels for 0%

profile of v1, /device:TPU:1, one launch (start us, length us, event | category | flops | bytes accessed | tf_op | source)
XLA Modules:
  0.0 329.8 jit_solution(4244768521233593421)
XLA Ops:
  8.0 1.9 pad_maximum_fusion
  9.9 3.4 %tile.4 = bf16[16,4,128,256]{3,2,1,0:T(8,128)(2,1)} broadcast(bf16[4,128,256]{2,1,0:T(8,128)(2,1)} %param.10), dimensions={1,2,3} | broadcast | bytes 4456448 | tf_op jit(solution)/shard_map/tile | solution.py:80
  13.3 10.0 %all-to-all-start = ((bf16[64,128,256]{2,1,0:T(8,128)(2,1)}), bf16[64,128,256]{2,1,0:T(8,128)(2,1)}, u32[]{:S(2)}, u32[]{:S(2)}) async-start(bf16[64,128,256]{2,1,0:T(8,128)(2,1)} %bitcast.182), calls=%async_computation | async-start | bytes 8388608 | tf_op jit(solution)/shard_map/all_to_all | solution.py:79
  23.4 47.0 %all-gather.6.cloned.1.call-done = bf16[512,4096]{1,0:T(8,128)(2,1)} async-done(((bf16[32,4096]{1,0:T(8,128)(2,1)}), bf16[512,4096]{1,0:T(8,128)(2,1)}) %all-gather.6.cloned.1.call-update) | async-done | bytes 4194320 | tf_op jit(solution)/shard_map/all_gather | solution.py:40
  70.4 4.1 %convolution_convert_fusion.1 = bf16[512,256]{1,0:T(8,128)(2,1)} fusion(bf16[512,4096]{1,0:T(8,128)(2,1)} %all-gather.6.cloned.1.call-done, bf16[4096,256]{1,0:T(8,128)(2,1)S(1)} %copy-done), kind=kOutput, calls=%fused_computation.56 | convolution fusion | flops 1073872896 | bytes 6553600 | tf_op jit(solution)/shard_map/dot_general | solution.py:41
  81.2 52.1 %all-to-all-done = bf16[64,128,256]{2,1,0:T(8,128)(2,1)} async-done(((bf16[64,128,256]{2,1,0:T(8,128)(2,1)}), bf16[64,128,256]{2,1,0:T(8,128)(2,1)}, u32[]{:S(2)}, u32[]{:S(2)}) %all-to-all-start) | async-done | bytes 4194336 | tf_op jit(solution)/shard_map/all_to_all | solution.py:79
  133.3 7.0 %reshape.123 = bf16[64,128,2,128]{3,2,1,0:T(2,128)(2,1)} reshape(bf16[64,128,256]{2,1,0:T(8,128)(2,1)} %all-to-all-done) | data formatting | bytes 8388608 | tf_op jit(solution)/shard_map/reshape | solution.py:93
  140.3 18.0 %all-gather.4.cloned.1.call-done = bf16[64,256,256]{2,1,0:T(8,128)(2,1)} async-done(((bf16[4,256,256]{2,1,0:T(8,128)(2,1)}), bf16[64,256,256]{2,1,0:T(8,128)(2,1)}) %all-gather.4.cloned.1.call-update) | async-done | bytes 8388624 | tf_op jit(solution)/shard_map/all_gather | solution.py:14
  158.3 6.0 %fusion.65 = (bf16[64,128,256]{2,1,0:T(8,128)(2,1)}, bf16[64,128,256]{2,1,0:T(8,128)(2,1)}) fusion(bf16[64,256,256]{2,1,0:T(8,128)(2,1)} %all-gather.4.cloned.1.call-done), kind=kLoop, calls=%fused_computation.91 | loop fusion | bytes 16777216 | tf_op jit(solution)/shard_map/split | solution.py:15
  164.4 2.9 gather_fusion.4
  167.3 3.0 reshape.118
  170.3 7.3 %copy.136 = bf16[4,12,128,2,128]{2,4,1,3,0:T(8,128)(2,1)S(1)} copy(bf16[4,12,128,2,128]{4,3,2,1,0:T(2,128)(2,1)} %reshape.118) | data formatting | bytes 6291456 | tf_op jit(solution)/shard_map/reshape | solution.py:45
  177.6 4.8 %gather_fusion.5 = bf16[48,128,256]{2,1,0:T(8,128)(2,1)} fusion(bf16[64,128,256]{2,1,0:T(8,128)(2,1)} %get-tuple-element.150, s32[1024]{0:T(1024)S(1)} %pad_clamp_fusion.1), kind=kCustom, calls=%fused_computation.5 | custom fusion | bytes 6291648 | tf_op jit(solution)/shard_map/gather | solution.py:46
  182.4 5.6 %reshape.121 = bf16[4,12,128,2,128]{4,3,2,1,0:T(2,128)(2,1)} reshape(bf16[48,128,256]{2,1,0:T(8,128)(2,1)} %gather_fusion.5) | data formatting | bytes 6291456 | tf_op jit(solution)/shard_map/reshape | solution.py:46
  188.0 8.7 %copy.133 = bf16[4,12,128,2,128]{2,4,1,3,0:T(8,128)(2,1)} copy(bf16[4,12,128,2,128]{4,3,2,1,0:T(2,128)(2,1)} %reshape.121) | data formatting | bytes 6291456 | tf_op jit(solution)/shard_map/reshape | solution.py:46
  196.6 1.9 select_reduce_fusion.1
  198.6 1.4 select_reduce_fusion
  200.0 1.8 copy-done.2
  202.8 2.4 multiply_reduce_fusion
  205.2 7.6 %fusion.45 = bf16[4,2,128,128]{3,2,1,0:T(8,128)(2,1)} fusion(bf16[4,12,128,2,128]{2,4,1,3,0:T(8,128)(2,1)S(1)} %copy.136, f32[4,2,12,128,128]{4,3,2,1,0:T(8,128)} %copy-done.2, f32[4,2,128]{2,1,0:T(2,128)S(1)} %get-tuple-element.160, f32[4,2,128]{2,1,0:T(2,128)S(1)} %bitcast.196, pred[4,12]{1,0:T(4,128)(4,1)S(1)} %copy.128, ...), kind=kOutput, calls=%fused_computation.55 | convolution fusion | flops 815005696 | bytes 13115440 | tf_op jit(solution)/shard_map/shajb,sjbhd->sahd/dot_general | solution.py:71
  212.8 1.8 copy.149
  215.7 16.2 %all_gather.14 = f32[64,4,128]{2,1,0:T(4,128)S(1)} all-gather(f32[4,4,128]{2,1,0:T(4,128)S(1)} %pad_maximum_fusion.1), channel_id=1, replica_groups=mesh['ctx'=16,'tp'=16] {'ctx'}, dimensions={0}, use_global_device_ids=true | all-gather | bytes 139264 | tf_op jit(solution)/shard_map/all_gather | solution.py:14
  232.6 4.8 %fusion.27 = bf16[4096,256]{0,1:T(8,128)(2,1)} fusion(bf16[512,4096]{1,0:T(8,128)(2,1)} %all-gather.6.cloned.1.call-done, bf16[64,8,2,128]{3,2,1,0:T(2,128)(2,1)S(1)} %bitcast.187), kind=kOutput, calls=%fused_computation.43 | convolution fusion | flops 1074790400 | bytes 6553600 | tf_op jit(solution)/shard_map/dot_general | solution.py:146
  237.4 7.0 %reshape.127 = bf16[64,128,2,128]{3,2,1,0:T(2,128)(2,1)} reshape(bf16[64,128,256]{2,1,0:T(8,128)(2,1)} %all-gather.8.cloned.1.call-done) | data formatting | bytes 8388608 | tf_op jit(solution)/shard_map/reshape | solution.py:94
  244.4 74.5 %while.12 = (s32[]{:T(128)}, bf16[4,128,2,128]{1,3,2,0:T(8,128)(2,1)S(1)}, bf16[4,128,2,128]{1,3,2,0:T(8,128)(2,1)}, s32[4,12]{1,0:T(4,128)S(1)}, bf16[64,128,2,...) while((s32[]{:T(128)}, ...), condition=%wide.region_8.9_spmd, body=%wide.region_7.8_spmd.sunk | while | flops 405505056 | bytes 14550529 | solution.py:139
  244.4 4.3 %gather_fusion = bf16[12,128,2,128]{3,2,1,0:T(2,128)(2,1)S(1)} fusion(bf16[64,128,2,128]{3,2,1,0:T(2,128)(2,1)} %get-tuple-element.257, s32[1024]{0:T(1024)S(1)} %pad_clamp_fusion.3), kind=kCustom, calls=%fused_computation.clone.1 | custom fusion | bytes 1572912 | tf_op jit(solution)/shard_map/while/body/eval_jaxpr/gather | solution.py:107
  249.5 1.4 gather_fusion.1
  252.3 5.3 %gather_fusion.2 = bf16[12,128,2,128]{3,2,1,0:T(2,128)(2,1)} fusion(bf16[64,128,2,128]{3,2,1,0:T(2,128)(2,1)} %get-tuple-element.262, s32[1024]{0:T(1024)S(1)} %pad_clamp_fusion.3), kind=kCustom, calls=%fused_computation.2.clone.1 | custom fusion | bytes 1572912 | tf_op jit(solution)/shard_map/while/body/eval_jaxpr/gather | solution.py:108
  257.6 2.3 copy.196
  260.5 1.5 fusion.100
  263.1 4.3 %gather_fusion = bf16[12,128,2,128]{3,2,1,0:T(2,128)(2,1)S(1)} fusion(bf16[64,128,2,128]{3,2,1,0:T(2,128)(2,1)} %get-tuple-element.257, s32[1024]{0:T(1024)S(1)} %pad_clamp_fusion.3), kind=kCustom, calls=%fused_computation.clone.1 | custom fusion | bytes 1572912 | tf_op jit(solution)/shard_map/while/body/eval_jaxpr/gather | solution.py:107
  268.1 1.4 gather_fusion.1
  269.6 1.3 fusion.99
  270.9 5.3 %gather_fusion.2 = bf16[12,128,2,128]{3,2,1,0:T(2,128)(2,1)} fusion(bf16[64,128,2,128]{3,2,1,0:T(2,128)(2,1)} %get-tuple-element.262, s32[1024]{0:T(1024)S(1)} %pad_clamp_fusion.3), kind=kCustom, calls=%fused_computation.2.clone.1 | custom fusion | bytes 1572912 | tf_op jit(solution)/shard_map/while/body/eval_jaxpr/gather | solution.py:108
  276.2 2.3 copy.196
  279.2 1.5 fusion.100
  281.7 4.3 %gather_fusion = bf16[12,128,2,128]{3,2,1,0:T(2,128)(2,1)S(1)} fusion(bf16[64,128,2,128]{3,2,1,0:T(2,128)(2,1)} %get-tuple-element.257, s32[1024]{0:T(1024)S(1)} %pad_clamp_fusion.3), kind=kCustom, calls=%fused_computation.clone.1 | custom fusion | bytes 1572912 | tf_op jit(solution)/shard_map/while/body/eval_jaxpr/gather | solution.py:107
  286.8 1.4 gather_fusion.1
  289.6 5.3 %gather_fusion.2 = bf16[12,128,2,128]{3,2,1,0:T(2,128)(2,1)} fusion(bf16[64,128,2,128]{3,2,1,0:T(2,128)(2,1)} %get-tuple-element.262, s32[1024]{0:T(1024)S(1)} %pad_clamp_fusion.3), kind=kCustom, calls=%fused_computation.2.clone.1 | custom fusion | bytes 1572912 | tf_op jit(solution)/shard_map/while/body/eval_jaxpr/gather | solution.py:108
  294.9 2.3 copy.196
  297.8 1.5 fusion.100
  300.3 4.3 %gather_fusion = bf16[12,128,2,128]{3,2,1,0:T(2,128)(2,1)S(1)} fusion(bf16[64,128,2,128]{3,2,1,0:T(2,128)(2,1)} %get-tuple-element.257, s32[1024]{0:T(1024)S(1)} %pad_clamp_fusion.3), kind=kCustom, calls=%fused_computation.clone.1 | custom fusion | bytes 1572912 | tf_op jit(solution)/shard_map/while/body/eval_jaxpr/gather | solution.py:107
  305.4 1.4 gather_fusion.1
  308.2 5.3 %gather_fusion.2 = bf16[12,128,2,128]{3,2,1,0:T(2,128)(2,1)} fusion(bf16[64,128,2,128]{3,2,1,0:T(2,128)(2,1)} %get-tuple-element.262, s32[1024]{0:T(1024)S(1)} %pad_clamp_fusion.3), kind=kCustom, calls=%fused_computation.2.clone.1 | custom fusion | bytes 1572912 | tf_op jit(solution)/shard_map/while/body/eval_jaxpr/gather | solution.py:108
  313.5 2.3 copy.196
  316.4 1.5 fusion.100
  319.8 1.8 copy.175
  321.6 1.7 copy.150
  (105 shorter events, 24.5 us)
Async XLA Ops:
  7.2 63.3 %copy-start = (bf16[4096,256]{1,0:T(8,128)(2,1)S(1)}, bf16[4096,256]{1,0:T(8,128)(2,1)}, u32[]{:S(2)}) copy-start(bf16[4096,256]{1,0:T(8,128)(2,1)} %param.14) | copy-start | bytes 6291460
  7.2 63.2 %all-gather.6.cloned.1.call-start = ((), (), s32[]{:S(2)}) async-start(), calls=%async_computation.3 | async-start | bytes 4456448 | tf_op jit(solution)/shard_map/all_gather | solution.py:40
  7.9 150.4 %all-gather.4.cloned.1.call-start = ((), (), s32[]{:S(2)}) async-start(), calls=%async_computation.2 | async-start | bytes 8912896 | tf_op jit(solution)/shard_map/all_gather | solution.py:14
  13.3 120.0 %all-to-all-start = ((bf16[64,128,256]{2,1,0:T(8,128)(2,1)}), bf16[64,128,256]{2,1,0:T(8,128)(2,1)}, u32[]{:S(2)}, u32[]{:S(2)}) async-start(bf16[64,128,256]{2,1,0:T(8,128)(2,1)} %bitcast.182), calls=%async_computation | async-start | bytes 8388608 | tf_op jit(solution)/shard_map/all_to_all | solution.py:79
  23.3 51.4 %copy-start.4 = (bf16[4,128,256]{2,1,0:T(8,128)(2,1)S(1)}, bf16[4,128,256]{2,1,0:T(8,128)(2,1)}, u32[]{:S(2)}) copy-start(bf16[4,128,256]{2,1,0:T(8,128)(2,1)} %param.10) | copy-start | bytes 786436
  23.3 51.5 %copy-start.7 = (bf16[4,128,256]{2,1,0:T(8,128)(2,1)S(1)}, bf16[4,128,256]{2,1,0:T(8,128)(2,1)}, u32[]{:S(2)}) copy-start(bf16[4,128,256]{2,1,0:T(8,128)(2,1)} %param.11) | copy-start | bytes 786436
  23.3 52.3 %copy-start.8 = (bf16[4,128,256]{2,1,0:T(8,128)(2,1)S(1)}, bf16[4,128,256]{2,1,0:T(8,128)(2,1)}, u32[]{:S(2)}) copy-start(bf16[4,128,256]{2,1,0:T(8,128)(2,1)} %param.12) | copy-start | bytes 786436
  23.3 53.1 %copy-start.11 = (s32[64]{0:T(128)S(1)}, s32[64]{0:T(128)}, u32[]{:S(2)}) copy-start(s32[64]{0:T(128)} %param.17) | copy-start | bytes 772
  23.3 53.1 %copy-start.12 = (s32[64,12]{0,1:T(8,128)S(1)}, s32[64,12]{0,1:T(8,128)}, u32[]{:S(2)}) copy-start(s32[64,12]{0,1:T(8,128)} %param.15) | copy-start | bytes 9220
  23.3 54.0 %copy-start.13 = (s32[64,12]{0,1:T(8,128)S(1)}, s32[64,12]{0,1:T(8,128)}, u32[]{:S(2)}) copy-start(s32[64,12]{0,1:T(8,128)} %param.16) | copy-start | bytes 9220
  23.3 214.1 %all-gather.8.cloned.1.call-start = ((), (), s32[]{:S(2)}) async-start(), calls=%async_computation.4 | async-start | bytes 4456448 | tf_op jit(solution)/shard_map/all_gather | solution.py:90
  74.6 247.0 %reduce-scatter.2.cloned.1.call-start = ((), (), s32[]{:S(2)}) async-start(), calls=%async_computation.5 | async-start | bytes 2228224 | tf_op jit(solution)/shard_map/reduce_scatter | solution.py:145
  80.0 60.3 %copy-start.5 = (bf16[4,128,2,128]{3,2,1,0:T(2,128)(2,1)}, bf16[4,128,2,128]{3,2,1,0:T(2,128)(2,1)S(1)}, u32[]{:S(2)}) copy-start(bf16[4,128,2,128]{3,2,1,0:T(2,128)(2,1)S(1)} %reshape.120) | copy-start | bytes 786436
  198.6 3.2 copy-start.2
  198.6 4.2 %copy-start.3 = (bf16[4,12,128,2,128]{2,4,1,3,0:T(8,128)(2,1)S(1)}, bf16[4,12,128,2,128]{2,4,1,3,0:T(8,128)(2,1)}, u32[]{:S(2)}) copy-start(bf16[4,12,128,2,128]{2,4,1,3,0:T(8,128)(2,1)} %copy.133) | copy-start | bytes 9437188
  198.6 4.2 %copy-start.9 = (f32[4,2,128,128]{2,3,1,0:T(8,128)S(1)}, f32[4,2,128,128]{2,3,1,0:T(8,128)}, u32[]{:S(2)}) copy-start(f32[4,2,128,128]{2,3,1,0:T(8,128)} %copy.167) | copy-start | bytes 1572868
  202.8 2.4 copy-start.6
  237.4 7.0 %copy-start.10 = (bf16[4,128,2,128]{1,3,2,0:T(8,128)(2,1)S(1)}, bf16[4,128,2,128]{1,3,2,0:T(8,128)(2,1)}, u32[]{:S(2)}) copy-start(bf16[4,128,2,128]{1,3,2,0:T(8,128)(2,1)} %custom-call.12) | copy-start | bytes 786436
  319.0 4.3 %copy-start.1 = (bf16[4096,256]{1,0:T(8,128)(2,1)S(1)}, bf16[4096,256]{1,0:T(8,128)(2,1)}, u32[]{:S(2)}) copy-start(bf16[4096,256]{1,0:T(8,128)(2,1)} %param.14) | copy-start | bytes 6291460
Sparse Core Ops, SparseCore 0:
  10.4 59.9 all-gather.5
  72.2 86.0 all-gather.3
  160.8 40.9 all-gather.7
  237.5 56.6 reduce-scatter.1
